TPU v7x, 256 devices: a whole 4x4x8 slice. The times are simulated.
256 devices in a mesh: row: 8 (over z_hi, x), col: 32 (over z_lo, y, core).
Axes of the slice: x: 4, y: 4, z: 8 (z_hi: 2, z_lo: 4; z = z_hi * 4 + z_lo), core: 2. Of those that a mesh axis runs over, the one named last changes fastest.
Arguments:
- region_factors: bfloat16 [262144, 512], P(('row', 'col')), may hold values from -1.25 to 1.25
- item_factors: bfloat16 [32, 128, 512], P('col', 'row'), may hold values from -1.25 to 1.25
- slab_blocks: bfloat16 [256, 32, 6, 128, 128], P(('row', 'col')), may hold values from -6 to 6
- block_rows: int32 [256, 32, 6], P(('row', 'col')), may hold values from 0 to 7, as said below
- counts: int32 [256, 32], P(('row', 'col')), may hold values from 1 to 6, as said below
Outputs:
- new_regions: float32 [262144, 512], P(('row', 'col'))
- new_items: float32 [32, 128, 512], P('col', 'row')
Inputs may be any that keep to these rules, and one draw needn't show every extreme that they name: `counts`: every entry is at least 1; some device-block has exactly 6 present blocks in some block column. `block_rows`: for each device-block and block column, the first counts[d, p] entries are distinct; entries at slots s >= counts[d, p] (and their slab blocks) are not used.
All inputs are finite; a program needn't handle non-finite values.
Results may differ from a plain program's by a relative error of at most 0.0023.
Values may be sent and summed in bfloat16 or wider, within the bound.
No kernel may reach another device: no remote copies, remote signals or barrier semaphores. Data moves between devices by JAX's collectives and lax.ppermute only.
A program may use at most 128 MiB of HBM per device.

v0:
```python
import jax
import jax.numpy as jnp
from jax import lax
from jax.sharding import PartitionSpec as P

region_rate = 0.05
item_rate = 0.01
decay_rate = 0.1


def passed_along(value, axis, steps):
    count = lax.axis_size(axis)
    pairs = [(source, (source + steps) % count) for source in range(count)]
    return lax.ppermute(value, axis, pairs)


def pass_panel(panel_now):
    return passed_along(panel_now, "col", 1)


def on_device(region_factors, item_factors, slab_blocks, block_rows, counts):
    cycle_size = lax.axis_size("col")
    position = lax.axis_index("col")
    block_size = slab_blocks.shape[-1]
    factor_width = region_factors.shape[-1]
    slot_total = slab_blocks.shape[2]
    row_blocks = region_factors.shape[0] // block_size
    region_blocks = region_factors.reshape(row_blocks, block_size, factor_width)
    tiles_all = slab_blocks[0]
    row_lists = block_rows[0]
    live_counts = counts[0]
    slot_ids = jnp.arange(slot_total, dtype=jnp.int32)
    panel_start = lax.all_gather(item_factors, "row", axis=1, tiled=True)[0]
    region_zero = jnp.zeros((row_blocks, block_size, factor_width), jnp.float32)
    item_zero = jnp.zeros((block_size, factor_width), jnp.float32)

    def padded_work(column, panel_now, region_totals):
        rows_now = lax.dynamic_index_in_dim(row_lists, column, 0, keepdims=False)
        tiles_now = lax.dynamic_index_in_dim(tiles_all, column, 0, keepdims=False)
        count_now = lax.dynamic_index_in_dim(live_counts, column, 0, keepdims=False)
        chosen = jnp.take(region_blocks, rows_now, axis=0)
        predicted = jnp.einsum("sik,jk->sij", chosen, panel_now, preferred_element_type=jnp.float32)
        present = slot_ids < count_now
        residual = jnp.where(present[:, None, None], predicted - tiles_now.astype(jnp.float32), 0.0)
        residual = residual.astype(jnp.bfloat16)
        update = jnp.einsum("sij,jk->sik", residual, panel_now, preferred_element_type=jnp.float32)
        region_totals = region_totals.at[rows_now].add(update)
        item_part = jnp.einsum("sij,sik->jk", residual, chosen, preferred_element_type=jnp.float32)
        return (region_totals, item_part)

    def block_work(column, panel_now, region_totals):
        return padded_work(column, panel_now, region_totals)

    last_column = (position + 1) % cycle_size

    def cycle_travel(passed, carried):
        panel_now, grad_now, region_totals = carried
        column = (position - passed) % cycle_size
        region_totals, item_part = block_work(column, panel_now, region_totals)
        grad_now = grad_now + item_part
        panel_now = pass_panel(panel_now)
        grad_now = passed_along(grad_now, "col", 1)
        return (panel_now, grad_now, region_totals)

    panel_now, grad_now, region_totals = lax.fori_loop(
        0, cycle_size - 1, cycle_travel, (panel_start, item_zero, region_zero)
    )
    region_totals, item_part = block_work(last_column, panel_now, region_totals)
    grad_home = passed_along(grad_now + item_part, "col", 1)
    own_piece = lax.psum_scatter(grad_home, "row", scatter_dimension=0, tiled=True)
    regions_wide = region_factors.astype(jnp.float32)
    region_grad = region_totals.reshape(row_blocks * block_size, factor_width)
    new_regions = regions_wide - region_rate * (region_grad + decay_rate * regions_wide)
    own_rows = item_factors[0].astype(jnp.float32)
    new_items = (own_rows - item_rate * (own_piece + decay_rate * own_rows))[None]
    return (new_regions, new_items)


def solution(mesh):
    return jax.shard_map(
        on_device,
        mesh=mesh,
        in_specs=(
            P(("row", "col"), None),
            P("col", "row", None),
            P(("row", "col"), None, None, None, None),
            P(("row", "col"), None, None),
            P(("row", "col"), None),
        ),
        out_specs=(P(("row", "col"), None), P("col", "row", None)),
        check_vma=False,
    )
```

profile of v0, /device:TPU:8, one launch (start us, length us, event | category | flops | bytes accessed | tf_op | source)
XLA Modules:
  0.0 607.2 jit_solution(15959370318166916743)
XLA Ops:
  11.0 46.2 %all_gather.3 = bf16[1,128,512]{2,1,0:T(8,128)(2,1)S(1)} all-gather(bf16[1,16,512]{2,1,0:T(8,128)(2,1)} %param.10), channel_id=1, replica_groups=mesh['row'=8,'col'=32] {'row'}, dimensions={1}, use_global_device_ids=true | all-gather | bytes 147456 | tf_op jit(solution)/shard_map/all_gather | solution.py:33
  61.5 430.5 %while.20 = (s32[]{:T(128)}, bf16[128,512]{1,0:T(8,128)(2,1)S(1)}, f32[128,512]{1,0:T(8,128)S(1)}, f32[8,128,512]{2,1,0:T(8,128)}, s32[]{:T(128)}, /*index=5*/s3...) while((s32[]{:T(128)}, bf16[128,512]{1,0:T(8,128)(2,1)S(1)}, ...), condition=%wide.region_2.4_spmd.clone, body=%wide.region_0.3_spmd.clone.sunk | while | flops 303629376 | bytes 12849738 | solution.py:65
  142.4 5.7 collective-permute-done.1
  156.7 5.7 collective-permute-done.1
  171.1 5.7 collective-permute-done.1
  199.7 5.7 collective-permute-done.1
  214.1 5.7 collective-permute-done.1
  228.4 5.7 collective-permute-done.1
  242.7 5.7 collective-permute-done.1
  271.4 5.7 collective-permute-done.1
  285.7 5.7 collective-permute-done.1
  300.1 5.7 collective-permute-done.1
  314.4 5.7 collective-permute-done.1
  328.7 5.7 collective-permute-done.1
  343.1 5.7 collective-permute-done.1
  357.4 5.7 collective-permute-done.1
  371.7 5.7 collective-permute-done.1
  386.1 5.7 collective-permute-done.1
  400.4 5.7 collective-permute-done.1
  414.7 5.7 collective-permute-done.1
  429.1 5.7 collective-permute-done.1
  443.4 5.7 collective-permute-done.1
  495.7 8.2 %collective-permute-done.2 = f32[128,512]{1,0:T(8,128)S(1)} collective-permute-done((f32[128,512]{1,0:T(8,128)S(1)}, f32[128,512]{1,0:T(8,128)S(1)}, u32[]{:S(2)}, u32[]{:S(2)}) %collective-permute-start.2) | collective-permute-done | bytes 262176 | tf_op jit(solution)/shard_map/ppermute | solution.py:14
  509.2 89.8 %reduce-scatter.2.cloned.1.call-done = f32[16,512]{1,0:T(8,128)} async-done(((f32[128,512]{1,0:T(8,128)}), f32[16,512]{1,0:T(8,128)}) %reduce-scatter.2.cloned.1.call-update) | async-done | bytes 32784 | tf_op jit(solution)/shard_map/reduce_scatter | solution.py:70
  (476 shorter events, 333.3 us)
Async XLA Ops:
  7.2 591.8 %reduce-scatter.2.cloned.1.call-start = ((), (), s32[]{:S(2)}) async-start(), calls=%async_computation.1 | async-start | bytes 294912 | tf_op jit(solution)/shard_map/reduce_scatter | solution.py:70
  61.5 10.3 %collective-permute-start = (bf16[128,512]{1,0:T(8,128)(2,1)S(1)}, bf16[128,512]{1,0:T(8,128)(2,1)S(1)}, u32[]{:S(2)}, u32[]{:S(2)}) collective-permute-start(bf16[128,512]{1,0:T(8,128)(2,1)S(1)} %copy.21), channel_id=1, source_target_pairs={{0,1},{1,2},{2,3},{3,4},{4,5},{5,6},{6,7},{7,8},{8,9},{9,10},{10,1... | collective-permute-start | bytes 393224 | tf_op jit(solution)/shard_map/while/body/eval_jaxpr/ppermute | solution.py:14
  71.9 10.3 %collective-permute-start = (bf16[128,512]{1,0:T(8,128)(2,1)S(1)}, bf16[128,512]{1,0:T(8,128)(2,1)S(1)}, u32[]{:S(2)}, u32[]{:S(2)}) collective-permute-start(bf16[128,512]{1,0:T(8,128)(2,1)S(1)} %copy.21), channel_id=1, source_target_pairs={{0,1},{1,2},{2,3},{3,4},{4,5},{5,6},{6,7},{7,8},{8,9},{9,10},{10,1... | collective-permute-start | bytes 393224 | tf_op jit(solution)/shard_map/while/body/eval_jaxpr/ppermute | solution.py:14
  82.4 10.3 %collective-permute-start = (bf16[128,512]{1,0:T(8,128)(2,1)S(1)}, bf16[128,512]{1,0:T(8,128)(2,1)S(1)}, u32[]{:S(2)}, u32[]{:S(2)}) collective-permute-start(bf16[128,512]{1,0:T(8,128)(2,1)S(1)} %copy.21), channel_id=1, source_target_pairs={{0,1},{1,2},{2,3},{3,4},{4,5},{5,6},{6,7},{7,8},{8,9},{9,10},{10,1... | collective-permute-start | bytes 393224 | tf_op jit(solution)/shard_map/while/body/eval_jaxpr/ppermute | solution.py:14
  92.8 11.1 %collective-permute-start = (bf16[128,512]{1,0:T(8,128)(2,1)S(1)}, bf16[128,512]{1,0:T(8,128)(2,1)S(1)}, u32[]{:S(2)}, u32[]{:S(2)}) collective-permute-start(bf16[128,512]{1,0:T(8,128)(2,1)S(1)} %copy.21), channel_id=1, source_target_pairs={{0,1},{1,2},{2,3},{3,4},{4,5},{5,6},{6,7},{7,8},{8,9},{9,10},{10,1... | collective-permute-start | bytes 393224 | tf_op jit(solution)/shard_map/while/body/eval_jaxpr/ppermute | solution.py:14
  105.1 11.3 %collective-permute-start = (bf16[128,512]{1,0:T(8,128)(2,1)S(1)}, bf16[128,512]{1,0:T(8,128)(2,1)S(1)}, u32[]{:S(2)}, u32[]{:S(2)}) collective-permute-start(bf16[128,512]{1,0:T(8,128)(2,1)S(1)} %copy.21), channel_id=1, source_target_pairs={{0,1},{1,2},{2,3},{3,4},{4,5},{5,6},{6,7},{7,8},{8,9},{9,10},{10,1... | collective-permute-start | bytes 393224 | tf_op jit(solution)/shard_map/while/body/eval_jaxpr/ppermute | solution.py:14
  109.5 9.9 %collective-permute-start.1 = (f32[128,512]{1,0:T(8,128)}, f32[128,512]{1,0:T(8,128)S(1)}, u32[]{:S(2)}, u32[]{:S(2)}) collective-permute-start(f32[128,512]{1,0:T(8,128)} %fusion.42), channel_id=1, source_target_pairs={{0,1},{1,2},{2,3},{3,4},{4,5},{5,6},{6,7},{7,8},{8,9},{9,10},{10,1... | collective-permute-start | bytes 786440 | tf_op jit(solution)/shard_map/while/body/eval_jaxpr/ppermute | solution.py:14
  123.8 9.9 %collective-permute-start.1 = (f32[128,512]{1,0:T(8,128)}, f32[128,512]{1,0:T(8,128)S(1)}, u32[]{:S(2)}, u32[]{:S(2)}) collective-permute-start(f32[128,512]{1,0:T(8,128)} %fusion.42), channel_id=1, source_target_pairs={{0,1},{1,2},{2,3},{3,4},{4,5},{5,6},{6,7},{7,8},{8,9},{9,10},{10,1... | collective-permute-start | bytes 786440 | tf_op jit(solution)/shard_map/while/body/eval_jaxpr/ppermute | solution.py:14
  138.1 9.9 %collective-permute-start.1 = (f32[128,512]{1,0:T(8,128)}, f32[128,512]{1,0:T(8,128)S(1)}, u32[]{:S(2)}, u32[]{:S(2)}) collective-permute-start(f32[128,512]{1,0:T(8,128)} %fusion.42), channel_id=1, source_target_pairs={{0,1},{1,2},{2,3},{3,4},{4,5},{5,6},{6,7},{7,8},{8,9},{9,10},{10,1... | collective-permute-start | bytes 786440 | tf_op jit(solution)/shard_map/while/body/eval_jaxpr/ppermute | solution.py:14
  152.5 9.9 %collective-permute-start.1 = (f32[128,512]{1,0:T(8,128)}, f32[128,512]{1,0:T(8,128)S(1)}, u32[]{:S(2)}, u32[]{:S(2)}) collective-permute-start(f32[128,512]{1,0:T(8,128)} %fusion.42), channel_id=1, source_target_pairs={{0,1},{1,2},{2,3},{3,4},{4,5},{5,6},{6,7},{7,8},{8,9},{9,10},{10,1... | collective-permute-start | bytes 786440 | tf_op jit(solution)/shard_map/while/body/eval_jaxpr/ppermute | solution.py:14
  166.8 9.9 %collective-permute-start.1 = (f32[128,512]{1,0:T(8,128)}, f32[128,512]{1,0:T(8,128)S(1)}, u32[]{:S(2)}, u32[]{:S(2)}) collective-permute-start(f32[128,512]{1,0:T(8,128)} %fusion.42), channel_id=1, source_target_pairs={{0,1},{1,2},{2,3},{3,4},{4,5},{5,6},{6,7},{7,8},{8,9},{9,10},{10,1... | collective-permute-start | bytes 786440 | tf_op jit(solution)/shard_map/while/body/eval_jaxpr/ppermute | solution.py:14
  181.1 9.9 %collective-permute-start.1 = (f32[128,512]{1,0:T(8,128)}, f32[128,512]{1,0:T(8,128)S(1)}, u32[]{:S(2)}, u32[]{:S(2)}) collective-permute-start(f32[128,512]{1,0:T(8,128)} %fusion.42), channel_id=1, source_target_pairs={{0,1},{1,2},{2,3},{3,4},{4,5},{5,6},{6,7},{7,8},{8,9},{9,10},{10,1... | collective-permute-start | bytes 786440 | tf_op jit(solution)/shard_map/while/body/eval_jaxpr/ppermute | solution.py:14
  195.5 9.9 %collective-permute-start.1 = (f32[128,512]{1,0:T(8,128)}, f32[128,512]{1,0:T(8,128)S(1)}, u32[]{:S(2)}, u32[]{:S(2)}) collective-permute-start(f32[128,512]{1,0:T(8,128)} %fusion.42), channel_id=1, source_target_pairs={{0,1},{1,2},{2,3},{3,4},{4,5},{5,6},{6,7},{7,8},{8,9},{9,10},{10,1... | collective-permute-start | bytes 786440 | tf_op jit(solution)/shard_map/while/body/eval_jaxpr/ppermute | solution.py:14
  209.8 9.9 %collective-permute-start.1 = (f32[128,512]{1,0:T(8,128)}, f32[128,512]{1,0:T(8,128)S(1)}, u32[]{:S(2)}, u32[]{:S(2)}) collective-permute-start(f32[128,512]{1,0:T(8,128)} %fusion.42), channel_id=1, source_target_pairs={{0,1},{1,2},{2,3},{3,4},{4,5},{5,6},{6,7},{7,8},{8,9},{9,10},{10,1... | collective-permute-start | bytes 786440 | tf_op jit(solution)/shard_map/while/body/eval_jaxpr/ppermute | solution.py:14
  224.1 9.9 %collective-permute-start.1 = (f32[128,512]{1,0:T(8,128)}, f32[128,512]{1,0:T(8,128)S(1)}, u32[]{:S(2)}, u32[]{:S(2)}) collective-permute-start(f32[128,512]{1,0:T(8,128)} %fusion.42), channel_id=1, source_target_pairs={{0,1},{1,2},{2,3},{3,4},{4,5},{5,6},{6,7},{7,8},{8,9},{9,10},{10,1... | collective-permute-start | bytes 786440 | tf_op jit(solution)/shard_map/while/body/eval_jaxpr/ppermute | solution.py:14
  238.5 9.9 %collective-permute-start.1 = (f32[128,512]{1,0:T(8,128)}, f32[128,512]{1,0:T(8,128)S(1)}, u32[]{:S(2)}, u32[]{:S(2)}) collective-permute-start(f32[128,512]{1,0:T(8,128)} %fusion.42), channel_id=1, source_target_pairs={{0,1},{1,2},{2,3},{3,4},{4,5},{5,6},{6,7},{7,8},{8,9},{9,10},{10,1... | collective-permute-start | bytes 786440 | tf_op jit(solution)/shard_map/while/body/eval_jaxpr/ppermute | solution.py:14
  252.8 9.9 %collective-permute-start.1 = (f32[128,512]{1,0:T(8,128)}, f32[128,512]{1,0:T(8,128)S(1)}, u32[]{:S(2)}, u32[]{:S(2)}) collective-permute-start(f32[128,512]{1,0:T(8,128)} %fusion.42), channel_id=1, source_target_pairs={{0,1},{1,2},{2,3},{3,4},{4,5},{5,6},{6,7},{7,8},{8,9},{9,10},{10,1... | collective-permute-start | bytes 786440 | tf_op jit(solution)/shard_map/while/body/eval_jaxpr/ppermute | solution.py:14
  267.1 9.9 %collective-permute-start.1 = (f32[128,512]{1,0:T(8,128)}, f32[128,512]{1,0:T(8,128)S(1)}, u32[]{:S(2)}, u32[]{:S(2)}) collective-permute-start(f32[128,512]{1,0:T(8,128)} %fusion.42), channel_id=1, source_target_pairs={{0,1},{1,2},{2,3},{3,4},{4,5},{5,6},{6,7},{7,8},{8,9},{9,10},{10,1... | collective-permute-start | bytes 786440 | tf_op jit(solution)/shard_map/while/body/eval_jaxpr/ppermute | solution.py:14
  295.8 9.9 %collective-permute-start.1 = (f32[128,512]{1,0:T(8,128)}, f32[128,512]{1,0:T(8,128)S(1)}, u32[]{:S(2)}, u32[]{:S(2)}) collective-permute-start(f32[128,512]{1,0:T(8,128)} %fusion.42), channel_id=1, source_target_pairs={{0,1},{1,2},{2,3},{3,4},{4,5},{5,6},{6,7},{7,8},{8,9},{9,10},{10,1... | collective-permute-start | bytes 786440 | tf_op jit(solution)/shard_map/while/body/eval_jaxpr/ppermute | solution.py:14
  324.5 9.9 %collective-permute-start.1 = (f32[128,512]{1,0:T(8,128)}, f32[128,512]{1,0:T(8,128)S(1)}, u32[]{:S(2)}, u32[]{:S(2)}) collective-permute-start(f32[128,512]{1,0:T(8,128)} %fusion.42), channel_id=1, source_target_pairs={{0,1},{1,2},{2,3},{3,4},{4,5},{5,6},{6,7},{7,8},{8,9},{9,10},{10,1... | collective-permute-start | bytes 786440 | tf_op jit(solution)/shard_map/while/body/eval_jaxpr/ppermute | solution.py:14
  353.1 9.9 %collective-permute-start.1 = (f32[128,512]{1,0:T(8,128)}, f32[128,512]{1,0:T(8,128)S(1)}, u32[]{:S(2)}, u32[]{:S(2)}) collective-permute-start(f32[128,512]{1,0:T(8,128)} %fusion.42), channel_id=1, source_target_pairs={{0,1},{1,2},{2,3},{3,4},{4,5},{5,6},{6,7},{7,8},{8,9},{9,10},{10,1... | collective-permute-start | bytes 786440 | tf_op jit(solution)/shard_map/while/body/eval_jaxpr/ppermute | solution.py:14
  396.1 9.9 %collective-permute-start.1 = (f32[128,512]{1,0:T(8,128)}, f32[128,512]{1,0:T(8,128)S(1)}, u32[]{:S(2)}, u32[]{:S(2)}) collective-permute-start(f32[128,512]{1,0:T(8,128)} %fusion.42), channel_id=1, source_target_pairs={{0,1},{1,2},{2,3},{3,4},{4,5},{5,6},{6,7},{7,8},{8,9},{9,10},{10,1... | collective-permute-start | bytes 786440 | tf_op jit(solution)/shard_map/while/body/eval_jaxpr/ppermute | solution.py:14
  424.8 9.9 %collective-permute-start.1 = (f32[128,512]{1,0:T(8,128)}, f32[128,512]{1,0:T(8,128)S(1)}, u32[]{:S(2)}, u32[]{:S(2)}) collective-permute-start(f32[128,512]{1,0:T(8,128)} %fusion.42), channel_id=1, source_target_pairs={{0,1},{1,2},{2,3},{3,4},{4,5},{5,6},{6,7},{7,8},{8,9},{9,10},{10,1... | collective-permute-start | bytes 786440 | tf_op jit(solution)/shard_map/while/body/eval_jaxpr/ppermute | solution.py:14
  453.5 9.9 %collective-permute-start.1 = (f32[128,512]{1,0:T(8,128)}, f32[128,512]{1,0:T(8,128)S(1)}, u32[]{:S(2)}, u32[]{:S(2)}) collective-permute-start(f32[128,512]{1,0:T(8,128)} %fusion.42), channel_id=1, source_target_pairs={{0,1},{1,2},{2,3},{3,4},{4,5},{5,6},{6,7},{7,8},{8,9},{9,10},{10,1... | collective-permute-start | bytes 786440 | tf_op jit(solution)/shard_map/while/body/eval_jaxpr/ppermute | solution.py:14
  (46 other events, 564.9 us)
Sparse Core Ops, SparseCore 0:
  504.7 94.2 reduce-scatter.1
where the time goes:
time: 610 us; the launch traced here: 607 us
  waiting for transfers between devices  248 us (41%)
  other arithmetic  149 us (24%)
  matrix products  87.9 us (14%)
  blocking collectives  46.2 us (8%)
  local copies, waits for them, and re-layouts  45.8 us (8%)
  between operations  14.2 us (2%)
  starting transfers between devices  13.6 us (2%)
    ppermute x63, waiting for transfers between devices, passed_along(): return lax.ppermute(value, axis, pairs)  159 us
    scatter-add x32, other arithmetic, padded_work(): region_totals = region_totals.at[rows_now].add(update)  124 us
    reduce_scatter x1, waiting for transfers between devices, on_device(): lax.psum_scatter(grad_home, 'row', scatter_dimension=0, tiled=True)  89.8 us
    all_gather x1, blocking collectives, on_device(): panel_start = lax.all_gather(item_factors, 'row', axis=1, tiled=True)[0]  46.2 us
    dot_general x32, matrix products, padded_work(): jnp.einsum('sik,jk->sij', chosen, panel_now, preferred_element_type=jnp.f...  43.1 us
    dot_general x32, matrix products, padded_work(): jnp.einsum('sij,sik->jk', residual, chosen, preferred_element_type=jnp.fl...  32.8 us
    gather x32, local copies, waits for them, and re-layouts, padded_work(): chosen = jnp.take(region_blocks, rows_now, axis=0)  21.3 us
    dynamic_slice x32, local copies, waits for them, and re-layouts, padded_work(): count_now = lax.dynamic_index_in_dim(live_counts, column, 0, keepdims=False)  20.1 us
  transfers between devices with their start and end apart: 64, of which 33 were waited for; matrix products, arithmetic and copies ran while one was open for 44% of the time, Pallas kernels for 0%

commit v1 on v0

--- a/solution.py
+++ b/solution.py
@@ -30,7 +30,9 @@
     row_lists = block_rows[0]
     live_counts = counts[0]
     slot_ids = jnp.arange(slot_total, dtype=jnp.int32)
-    panel_start = lax.all_gather(item_factors, "row", axis=1, tiled=True)[0]
+    panel_start = jnp.concatenate(
+        lax.all_to_all(jnp.stack([item_factors] * lax.axis_size("row")), "row", 0, 0), axis=1
+    )[0]
     region_zero = jnp.zeros((row_blocks, block_size, factor_width), jnp.float32)
     item_zero = jnp.zeros((block_size, factor_width), jnp.float32)
 

time: 610 us -> 580 us (0.951)
  blocking collectives: 46.2 us -> 0 us
  starting transfers between devices: 13.6 us -> 25.2 us
    all_gather x1 -> x0, blocking collectives: 46.2 us -> none  [on_device(): panel_start = lax.all_gather(item_factors, 'row', axis=1, tiled=True)[0]]
    all_to_all x0 -> x1, starting transfers between devices: none -> 11.1 us  [on_device(): lax.all_to_all(jnp.stack([item_factors] * lax.axis_size('row')), 'row', 0...]
  transfers between devices with their start and end apart: 64 -> 65, of which waited for: 33 -> 34; matrix products, arithmetic and copies ran while one was open for 44% -> 48% of each run, Pallas kernels for 0% -> 0%
where the time goes in v1:
time: 580 us; the launch traced here: 577 us
  waiting for transfers between devices  248 us (43%)
  other arithmetic  150 us (26%)
  matrix products  88.9 us (15%)
  local copies, waits for them, and re-layouts  48.7 us (8%)
  starting transfers between devices  25.2 us (4%)
  between operations  14.1 us (2%)
    ppermute x63, waiting for transfers between devices, passed_along(): return lax.ppermute(value, axis, pairs)  159 us
    scatter-add x32, other arithmetic, padded_work(): region_totals = region_totals.at[rows_now].add(update)  124 us
    reduce_scatter x1, waiting for transfers between devices, on_device(): lax.psum_scatter(grad_home, 'row', scatter_dimension=0, tiled=True)  84.7 us
    dot_general x32, matrix products, padded_work(): jnp.einsum('sik,jk->sij', chosen, panel_now, preferred_element_type=jnp.f...  43.1 us
    dot_general x32, matrix products, padded_work(): jnp.einsum('sij,sik->jk', residual, chosen, preferred_element_type=jnp.fl...  32.9 us
    dynamic_slice x32, local copies, waits for them, and re-layouts, padded_work(): count_now = lax.dynamic_index_in_dim(live_counts, column, 0, keepdims=False)  21.5 us
    gather x32, local copies, waits for them, and re-layouts, padded_work(): chosen = jnp.take(region_blocks, rows_now, axis=0)  21.3 us
    lt x31, other arithmetic, padded_work(): present = slot_ids < count_now  20.9 us
  transfers between devices with their start and end apart: 65, of which 34 were waited for; matrix products, arithmetic and copies ran while one was open for 48% of the time, Pallas kernels for 0%

profile of v1, /device:TPU:8, one launch (start us, length us, event | category | flops | bytes accessed | tf_op | source)
XLA Modules:
  0.0 577.4 jit_solution(1041018516621986855)
XLA Ops:
  8.6 11.1 %all-to-all-start = ((bf16[8,1,16,512]{3,2,1,0:T(8,128)(2,1)}), bf16[8,1,16,512]{3,2,1,0:T(8,128)(2,1)S(1)}, u32[]{:S(2)}, u32[]{:S(2)}) async-start(bf16[8,1,16,512]{3,2,1,0:T(8,128)(2,1)} %stack.2), calls=%async_computation | async-start | bytes 262144 | tf_op jit(solution)/shard_map/all_to_all | solution.py:34
  31.7 433.0 %while.20 = (s32[]{:T(128)}, bf16[128,512]{1,0:T(8,128)(2,1)S(1)}, f32[128,512]{1,0:T(8,128)S(1)}, f32[8,128,512]{2,1,0:T(8,128)}, s32[]{:T(128)}, /*index=5*/s3...) while((s32[]{:T(128)}, bf16[128,512]{1,0:T(8,128)(2,1)S(1)}, ...), condition=%wide.region_2.4_spmd.clone, body=%wide.region_0.3_spmd.clone.sunk | while | flops 303629376 | bytes 12849738 | solution.py:67
  113.2 5.7 collective-permute-done.1
  127.6 5.6 collective-permute-done.1
  142.0 5.7 collective-permute-done.1
  170.8 5.7 collective-permute-done.1
  185.3 5.6 collective-permute-done.1
  199.7 5.7 collective-permute-done.1
  214.1 5.6 collective-permute-done.1
  228.5 5.7 collective-permute-done.1
  242.9 5.6 collective-permute-done.1
  257.3 5.7 collective-permute-done.1
  286.1 5.7 collective-permute-done.1
  300.6 5.6 collective-permute-done.1
  315.0 5.7 collective-permute-done.1
  343.8 5.7 collective-permute-done.1
  358.2 5.6 collective-permute-done.1
  372.6 5.7 collective-permute-done.1
  387.0 5.6 collective-permute-done.1
  401.4 5.7 collective-permute-done.1
  430.3 5.7 collective-permute-done.1
  459.1 5.7 collective-permute-done.1
  467.1 9.7 %collective-permute-done.2 = f32[128,512]{1,0:T(8,128)S(1)} collective-permute-done((f32[128,512]{1,0:T(8,128)S(1)}, f32[128,512]{1,0:T(8,128)S(1)}, u32[]{:S(2)}, u32[]{:S(2)}) %collective-permute-start.2) | collective-permute-done | bytes 262176 | tf_op jit(solution)/shard_map/ppermute | solution.py:14
  484.5 84.7 %reduce-scatter.2.cloned.1.call-done = f32[16,512]{1,0:T(8,128)} async-done(((f32[128,512]{1,0:T(8,128)}), f32[16,512]{1,0:T(8,128)}) %reduce-scatter.2.cloned.1.call-update) | async-done | bytes 32784 | tf_op jit(solution)/shard_map/reduce_scatter | solution.py:72
  (480 shorter events, 342.3 us)
Async XLA Ops:
  8.6 21.5 %all-to-all-start = ((bf16[8,1,16,512]{3,2,1,0:T(8,128)(2,1)}), bf16[8,1,16,512]{3,2,1,0:T(8,128)(2,1)S(1)}, u32[]{:S(2)}, u32[]{:S(2)}) async-start(bf16[8,1,16,512]{3,2,1,0:T(8,128)(2,1)} %stack.2), calls=%async_computation | async-start | bytes 262144 | tf_op jit(solution)/shard_map/all_to_all | solution.py:34
  19.6 549.6 %reduce-scatter.2.cloned.1.call-start = ((), (), s32[]{:S(2)}) async-start(), calls=%async_computation.2 | async-start | bytes 294912 | tf_op jit(solution)/shard_map/reduce_scatter | solution.py:72
  31.7 10.4 %collective-permute-start = (bf16[128,512]{1,0:T(8,128)(2,1)S(1)}, bf16[128,512]{1,0:T(8,128)(2,1)S(1)}, u32[]{:S(2)}, u32[]{:S(2)}) collective-permute-start(bf16[128,512]{1,0:T(8,128)(2,1)S(1)} %copy.24), channel_id=1, source_target_pairs={{0,1},{1,2},{2,3},{3,4},{4,5},{5,6},{6,7},{7,8},{8,9},{9,10},{10,1... | collective-permute-start | bytes 393224 | tf_op jit(solution)/shard_map/while/body/eval_jaxpr/ppermute | solution.py:14
  42.2 10.4 %collective-permute-start = (bf16[128,512]{1,0:T(8,128)(2,1)S(1)}, bf16[128,512]{1,0:T(8,128)(2,1)S(1)}, u32[]{:S(2)}, u32[]{:S(2)}) collective-permute-start(bf16[128,512]{1,0:T(8,128)(2,1)S(1)} %copy.24), channel_id=1, source_target_pairs={{0,1},{1,2},{2,3},{3,4},{4,5},{5,6},{6,7},{7,8},{8,9},{9,10},{10,1... | collective-permute-start | bytes 393224 | tf_op jit(solution)/shard_map/while/body/eval_jaxpr/ppermute | solution.py:14
  52.7 10.4 %collective-permute-start = (bf16[128,512]{1,0:T(8,128)(2,1)S(1)}, bf16[128,512]{1,0:T(8,128)(2,1)S(1)}, u32[]{:S(2)}, u32[]{:S(2)}) collective-permute-start(bf16[128,512]{1,0:T(8,128)(2,1)S(1)} %copy.24), channel_id=1, source_target_pairs={{0,1},{1,2},{2,3},{3,4},{4,5},{5,6},{6,7},{7,8},{8,9},{9,10},{10,1... | collective-permute-start | bytes 393224 | tf_op jit(solution)/shard_map/while/body/eval_jaxpr/ppermute | solution.py:14
  63.2 11.4 %collective-permute-start = (bf16[128,512]{1,0:T(8,128)(2,1)S(1)}, bf16[128,512]{1,0:T(8,128)(2,1)S(1)}, u32[]{:S(2)}, u32[]{:S(2)}) collective-permute-start(bf16[128,512]{1,0:T(8,128)(2,1)S(1)} %copy.24), channel_id=1, source_target_pairs={{0,1},{1,2},{2,3},{3,4},{4,5},{5,6},{6,7},{7,8},{8,9},{9,10},{10,1... | collective-permute-start | bytes 393224 | tf_op jit(solution)/shard_map/while/body/eval_jaxpr/ppermute | solution.py:14
  75.6 11.6 %collective-permute-start = (bf16[128,512]{1,0:T(8,128)(2,1)S(1)}, bf16[128,512]{1,0:T(8,128)(2,1)S(1)}, u32[]{:S(2)}, u32[]{:S(2)}) collective-permute-start(bf16[128,512]{1,0:T(8,128)(2,1)S(1)} %copy.24), channel_id=1, source_target_pairs={{0,1},{1,2},{2,3},{3,4},{4,5},{5,6},{6,7},{7,8},{8,9},{9,10},{10,1... | collective-permute-start | bytes 393224 | tf_op jit(solution)/shard_map/while/body/eval_jaxpr/ppermute | solution.py:14
  80.1 9.9 %collective-permute-start.1 = (f32[128,512]{1,0:T(8,128)}, f32[128,512]{1,0:T(8,128)S(1)}, u32[]{:S(2)}, u32[]{:S(2)}) collective-permute-start(f32[128,512]{1,0:T(8,128)} %fusion.42), channel_id=1, source_target_pairs={{0,1},{1,2},{2,3},{3,4},{4,5},{5,6},{6,7},{7,8},{8,9},{9,10},{10,1... | collective-permute-start | bytes 786440 | tf_op jit(solution)/shard_map/while/body/eval_jaxpr/ppermute | solution.py:14
  108.9 9.9 %collective-permute-start.1 = (f32[128,512]{1,0:T(8,128)}, f32[128,512]{1,0:T(8,128)S(1)}, u32[]{:S(2)}, u32[]{:S(2)}) collective-permute-start(f32[128,512]{1,0:T(8,128)} %fusion.42), channel_id=1, source_target_pairs={{0,1},{1,2},{2,3},{3,4},{4,5},{5,6},{6,7},{7,8},{8,9},{9,10},{10,1... | collective-permute-start | bytes 786440 | tf_op jit(solution)/shard_map/while/body/eval_jaxpr/ppermute | solution.py:14
  123.3 9.9 %collective-permute-start.1 = (f32[128,512]{1,0:T(8,128)}, f32[128,512]{1,0:T(8,128)S(1)}, u32[]{:S(2)}, u32[]{:S(2)}) collective-permute-start(f32[128,512]{1,0:T(8,128)} %fusion.42), channel_id=1, source_target_pairs={{0,1},{1,2},{2,3},{3,4},{4,5},{5,6},{6,7},{7,8},{8,9},{9,10},{10,1... | collective-permute-start | bytes 786440 | tf_op jit(solution)/shard_map/while/body/eval_jaxpr/ppermute | solution.py:14
  137.7 9.9 %collective-permute-start.1 = (f32[128,512]{1,0:T(8,128)}, f32[128,512]{1,0:T(8,128)S(1)}, u32[]{:S(2)}, u32[]{:S(2)}) collective-permute-start(f32[128,512]{1,0:T(8,128)} %fusion.42), channel_id=1, source_target_pairs={{0,1},{1,2},{2,3},{3,4},{4,5},{5,6},{6,7},{7,8},{8,9},{9,10},{10,1... | collective-permute-start | bytes 786440 | tf_op jit(solution)/shard_map/while/body/eval_jaxpr/ppermute | solution.py:14
  152.2 9.9 %collective-permute-start.1 = (f32[128,512]{1,0:T(8,128)}, f32[128,512]{1,0:T(8,128)S(1)}, u32[]{:S(2)}, u32[]{:S(2)}) collective-permute-start(f32[128,512]{1,0:T(8,128)} %fusion.42), channel_id=1, source_target_pairs={{0,1},{1,2},{2,3},{3,4},{4,5},{5,6},{6,7},{7,8},{8,9},{9,10},{10,1... | collective-permute-start | bytes 786440 | tf_op jit(solution)/shard_map/while/body/eval_jaxpr/ppermute | solution.py:14
  166.6 9.9 %collective-permute-start.1 = (f32[128,512]{1,0:T(8,128)}, f32[128,512]{1,0:T(8,128)S(1)}, u32[]{:S(2)}, u32[]{:S(2)}) collective-permute-start(f32[128,512]{1,0:T(8,128)} %fusion.42), channel_id=1, source_target_pairs={{0,1},{1,2},{2,3},{3,4},{4,5},{5,6},{6,7},{7,8},{8,9},{9,10},{10,1... | collective-permute-start | bytes 786440 | tf_op jit(solution)/shard_map/while/body/eval_jaxpr/ppermute | solution.py:14
  181.0 9.9 %collective-permute-start.1 = (f32[128,512]{1,0:T(8,128)}, f32[128,512]{1,0:T(8,128)S(1)}, u32[]{:S(2)}, u32[]{:S(2)}) collective-permute-start(f32[128,512]{1,0:T(8,128)} %fusion.42), channel_id=1, source_target_pairs={{0,1},{1,2},{2,3},{3,4},{4,5},{5,6},{6,7},{7,8},{8,9},{9,10},{10,1... | collective-permute-start | bytes 786440 | tf_op jit(solution)/shard_map/while/body/eval_jaxpr/ppermute | solution.py:14
  195.4 9.9 %collective-permute-start.1 = (f32[128,512]{1,0:T(8,128)}, f32[128,512]{1,0:T(8,128)S(1)}, u32[]{:S(2)}, u32[]{:S(2)}) collective-permute-start(f32[128,512]{1,0:T(8,128)} %fusion.42), channel_id=1, source_target_pairs={{0,1},{1,2},{2,3},{3,4},{4,5},{5,6},{6,7},{7,8},{8,9},{9,10},{10,1... | collective-permute-start | bytes 786440 | tf_op jit(solution)/shard_map/while/body/eval_jaxpr/ppermute | solution.py:14
  224.2 9.9 %collective-permute-start.1 = (f32[128,512]{1,0:T(8,128)}, f32[128,512]{1,0:T(8,128)S(1)}, u32[]{:S(2)}, u32[]{:S(2)}) collective-permute-start(f32[128,512]{1,0:T(8,128)} %fusion.42), channel_id=1, source_target_pairs={{0,1},{1,2},{2,3},{3,4},{4,5},{5,6},{6,7},{7,8},{8,9},{9,10},{10,1... | collective-permute-start | bytes 786440 | tf_op jit(solution)/shard_map/while/body/eval_jaxpr/ppermute | solution.py:14
  253.0 9.9 %collective-permute-start.1 = (f32[128,512]{1,0:T(8,128)}, f32[128,512]{1,0:T(8,128)S(1)}, u32[]{:S(2)}, u32[]{:S(2)}) collective-permute-start(f32[128,512]{1,0:T(8,128)} %fusion.42), channel_id=1, source_target_pairs={{0,1},{1,2},{2,3},{3,4},{4,5},{5,6},{6,7},{7,8},{8,9},{9,10},{10,1... | collective-permute-start | bytes 786440 | tf_op jit(solution)/shard_map/while/body/eval_jaxpr/ppermute | solution.py:14
  281.9 9.9 %collective-permute-start.1 = (f32[128,512]{1,0:T(8,128)}, f32[128,512]{1,0:T(8,128)S(1)}, u32[]{:S(2)}, u32[]{:S(2)}) collective-permute-start(f32[128,512]{1,0:T(8,128)} %fusion.42), channel_id=1, source_target_pairs={{0,1},{1,2},{2,3},{3,4},{4,5},{5,6},{6,7},{7,8},{8,9},{9,10},{10,1... | collective-permute-start | bytes 786440 | tf_op jit(solution)/shard_map/while/body/eval_jaxpr/ppermute | solution.py:14
  310.7 9.9 %collective-permute-start.1 = (f32[128,512]{1,0:T(8,128)}, f32[128,512]{1,0:T(8,128)S(1)}, u32[]{:S(2)}, u32[]{:S(2)}) collective-permute-start(f32[128,512]{1,0:T(8,128)} %fusion.42), channel_id=1, source_target_pairs={{0,1},{1,2},{2,3},{3,4},{4,5},{5,6},{6,7},{7,8},{8,9},{9,10},{10,1... | collective-permute-start | bytes 786440 | tf_op jit(solution)/shard_map/while/body/eval_jaxpr/ppermute | solution.py:14
  339.5 9.9 %collective-permute-start.1 = (f32[128,512]{1,0:T(8,128)}, f32[128,512]{1,0:T(8,128)S(1)}, u32[]{:S(2)}, u32[]{:S(2)}) collective-permute-start(f32[128,512]{1,0:T(8,128)} %fusion.42), channel_id=1, source_target_pairs={{0,1},{1,2},{2,3},{3,4},{4,5},{5,6},{6,7},{7,8},{8,9},{9,10},{10,1... | collective-permute-start | bytes 786440 | tf_op jit(solution)/shard_map/while/body/eval_jaxpr/ppermute | solution.py:14
  368.3 9.9 %collective-permute-start.1 = (f32[128,512]{1,0:T(8,128)}, f32[128,512]{1,0:T(8,128)S(1)}, u32[]{:S(2)}, u32[]{:S(2)}) collective-permute-start(f32[128,512]{1,0:T(8,128)} %fusion.42), channel_id=1, source_target_pairs={{0,1},{1,2},{2,3},{3,4},{4,5},{5,6},{6,7},{7,8},{8,9},{9,10},{10,1... | collective-permute-start | bytes 786440 | tf_op jit(solution)/shard_map/while/body/eval_jaxpr/ppermute | solution.py:14
  397.2 9.9 %collective-permute-start.1 = (f32[128,512]{1,0:T(8,128)}, f32[128,512]{1,0:T(8,128)S(1)}, u32[]{:S(2)}, u32[]{:S(2)}) collective-permute-start(f32[128,512]{1,0:T(8,128)} %fusion.42), channel_id=1, source_target_pairs={{0,1},{1,2},{2,3},{3,4},{4,5},{5,6},{6,7},{7,8},{8,9},{9,10},{10,1... | collective-permute-start | bytes 786440 | tf_op jit(solution)/shard_map/while/body/eval_jaxpr/ppermute | solution.py:14
  426.0 9.9 %collective-permute-start.1 = (f32[128,512]{1,0:T(8,128)}, f32[128,512]{1,0:T(8,128)S(1)}, u32[]{:S(2)}, u32[]{:S(2)}) collective-permute-start(f32[128,512]{1,0:T(8,128)} %fusion.42), channel_id=1, source_target_pairs={{0,1},{1,2},{2,3},{3,4},{4,5},{5,6},{6,7},{7,8},{8,9},{9,10},{10,1... | collective-permute-start | bytes 786440 | tf_op jit(solution)/shard_map/while/body/eval_jaxpr/ppermute | solution.py:14
  454.8 9.9 %collective-permute-start.1 = (f32[128,512]{1,0:T(8,128)}, f32[128,512]{1,0:T(8,128)S(1)}, u32[]{:S(2)}, u32[]{:S(2)}) collective-permute-start(f32[128,512]{1,0:T(8,128)} %fusion.42), channel_id=1, source_target_pairs={{0,1},{1,2},{2,3},{3,4},{4,5},{5,6},{6,7},{7,8},{8,9},{9,10},{10,1... | collective-permute-start | bytes 786440 | tf_op jit(solution)/shard_map/while/body/eval_jaxpr/ppermute | solution.py:14
  (48 other events, 512.7 us)
Sparse Core Ops, SparseCore 0:
  477.6 91.5 reduce-scatter.1
